TPU v7x, 32 devices: a whole 2x2x4 slice. The times are simulated.
32 devices in a mesh: clique: 8 (over z, core), shard: 4 (over y, x).
Axes of the slice: x: 2, y: 2, z: 4, core: 2. Of those that a mesh axis runs over, the one named last changes fastest.
Arguments:
- tables: float32 [3, 8, 4096, 128], P(None, 'clique', 'shard'), may hold values from 0.1 to 10
- up_map: int32 [2, 8, 4096], P(None, 'clique', 'shard'), may hold values from 0 to 4095, as said below
- down_map: int32 [2, 8, 4096], P(None, 'clique', 'shard'), may hold values from 0 to 4095, as said below
- parents: int32 [2, 8], replicated, may hold values from 0 to 7
Outputs:
- calibrated: float32 [3, 8, 4096, 128], P(None, 'clique', 'shard')
Inputs may be any that keep to these rules, and one draw needn't show every extreme that they name: For every edge and clique, of the 1024 blocks of one device exactly 256 name blocks in each range [k * 1024, (k + 1) * 1024). Every list of up_map and down_map names the same set of separator blocks; a named separator block is named by the same number of blocks of a clique in every list, a multiple of 1. For every edge and clique, of the 1024 blocks of one device exactly 256 name blocks in each range [k * 1024, (k + 1) * 1024). Every list of up_map and down_map names the same set of separator blocks; a named separator block is named by the same number of blocks of a clique in every list, a multiple of 1.
All inputs are finite; a program needn't handle non-finite values.
Results may differ from a plain program's by a relative error of at most 0.0003.
Values sent between devices are 32-bit elements; how exact they have to be, the bound alone decides.
No kernel may reach another device: no remote copies, remote signals or barrier semaphores. Data moves between devices by JAX's collectives and lax.ppermute only.
A program may use at most 64 MiB of HBM per device.

v0:
```python
import jax
import jax.numpy as jnp
from jax import lax
from jax.sharding import PartitionSpec as P

SEPB = 4096


def shards(tables, up_map, down_map, parents):
    shard_count = lax.axis_size("shard")
    clique_count = lax.axis_size("clique")
    block_count = tables.shape[2]
    lane_count = tables.shape[3]
    per_owner = SEPB // shard_count
    per_peer = block_count // shard_count
    sep_states = float(SEPB * lane_count)
    slot_ids = jnp.arange(per_owner, dtype=jnp.int32)

    def to_owners(potential, index_list):
        ordering = jnp.argsort(index_list // per_owner, stable=True)
        sent_rows = potential[ordering].reshape(shard_count, per_peer, lane_count)
        sent_slots = (index_list % per_owner)[ordering].reshape(shard_count, per_peer)
        arrived_rows, arrived_slots = (
            lax.all_to_all(sent_rows, "shard", split_axis=0, concat_axis=0, tiled=True),
            lax.all_to_all(sent_slots, "shard", split_axis=0, concat_axis=0, tiled=True),
        )
        one_hot = (arrived_slots.reshape(block_count)[:, None] == slot_ids[None, :]).astype(
            jnp.float32
        )
        message = jnp.dot(
            one_hot.T,
            arrived_rows.reshape(block_count, lane_count),
            precision=lax.Precision.HIGHEST,
            preferred_element_type=jnp.float32,
        )
        partial_sum = jnp.sum(message)
        total = lax.psum(partial_sum, "shard")
        return message * (sep_states / total)

    def fetch(owned_rows, index_list):
        gathered = lax.all_gather(owned_rows, "shard", axis=0, tiled=True)
        result = gathered[index_list]
        return result

    def route(owned_rows, mixing):
        pieces = owned_rows.reshape(clique_count, per_owner // clique_count, lane_count)
        combined = jnp.einsum(
            "oi,ixl->oxl",
            mixing,
            lax.all_to_all(pieces, "clique", split_axis=0, concat_axis=0, tiled=True),
            precision=lax.Precision.HIGHEST,
        )
        moved = lax.all_to_all(combined, "clique", split_axis=0, concat_axis=0, tiled=True)
        return moved.reshape(per_owner, lane_count)

    clique_ids = jnp.arange(clique_count, dtype=jnp.int32)
    current = [tables[0, 0], tables[1, 0], tables[2, 0]]
    previous = [tables[0, 0], tables[0, 0]]
    for edge in (1, 0):
        selector = (parents[edge][:, None] == clique_ids[None, :]).astype(jnp.float32)
        scaled = to_owners(current[edge + 1], up_map[edge, 0])
        previous[edge] = scaled
        incoming = jnp.exp(route(jnp.log(scaled), selector.T))
        current[edge] = current[edge] * fetch(incoming, down_map[edge, 0])
    for edge in (0, 1):
        selector = (parents[edge][:, None] == clique_ids[None, :]).astype(jnp.float32)
        fresh = to_owners(current[edge], down_map[edge, 0])
        from_parent = route(fresh, selector)
        update = from_parent / previous[edge]
        current[edge + 1] = current[edge + 1] * fetch(update, up_map[edge, 0])
    return jnp.stack(current)[:, None]


def solution(mesh):
    return jax.shard_map(
        shards,
        mesh=mesh,
        in_specs=(
            P(None, "clique", "shard", None),
            P(None, "clique", "shard"),
            P(None, "clique", "shard"),
            P(),
        ),
        out_specs=P(None, "clique", "shard", None),
        check_vma=False,
    )
```

profile of v0, /device:TPU:0, one launch (start us, length us, event | category | flops | bytes accessed | tf_op | source)
XLA Modules:
  0.0 467.1 jit_solution(16538825504890834248)
XLA Ops:
  7.3 4.4 sort.60
  11.6 8.8 %gather_fusion.1 = s32[1024]{0:T(1024)} fusion(s32[1024]{0:T(1024)S(1)} %get-tuple-element.30, s32[1024]{0:T(1024)S(1)} %fusion.17), kind=kCustom, calls=%fused_computation.1 | custom fusion | bytes 12288 | tf_op jit(solution)/shard_map/gather | solution.py:22
  20.5 5.2 %all-to-all-start.1 = ((s32[4,1,256]{2,1,0:T(1,128)}), s32[4,1,256]{2,1,0:T(1,128)S(1)}, u32[]{:S(2)}, u32[]{:S(2)}) async-start(s32[4,1,256]{2,1,0:T(1,128)} %bitcast.10), calls=%async_computation.1 | async-start | bytes 8192 | tf_op jit(solution)/shard_map/all_to_all | solution.py:25
  25.7 2.8 gather_fusion.2
  28.5 1.8 all-to-all-done.1
  30.3 10.1 %all_to_all.96 = f32[4,256,128]{2,1,0:T(8,128)S(1)} all-to-all(f32[4,256,128]{2,1,0:T(8,128)S(1)} %bitcast.91), channel_id=1, replica_groups=mesh['clique'=8,'shard'=4] {'shard'}, dimensions={0} | all-to-all | bytes 1048576 | tf_op jit(solution)/shard_map/all_to_all | solution.py:24
  40.5 4.2 fusion.40
  44.7 9.0 %psum.28 = f32[]{:T(128)} all-reduce(f32[]{:T(128)} %get-tuple-element.34), channel_id=1, replica_groups=mesh['clique'=8,'shard'=4] {'shard'}, use_global_device_ids=true, to_apply=%region_3.4 | all-reduce | flops 1 | bytes 8 | tf_op jit(solution)/shard_map/psum | solution.py:37
  55.2 4.9 %all-to-all-start.3 = ((f32[8,128,128]{2,1,0:T(8,128)}), f32[8,128,128]{2,1,0:T(8,128)S(1)}, u32[]{:S(2)}, u32[]{:S(2)}) async-start(f32[8,128,128]{2,1,0:T(8,128)} %bitcast.15), calls=%async_computation.3 | async-start | bytes 1048576 | tf_op jit(solution)/shard_map/all_to_all | solution.py:50
  60.2 15.3 %all-to-all-done.3 = f32[8,128,128]{2,1,0:T(8,128)S(1)} async-done(((f32[8,128,128]{2,1,0:T(8,128)}), f32[8,128,128]{2,1,0:T(8,128)S(1)}, u32[]{:S(2)}, u32[]{:S(2)}) %all-to-all-start.3) | async-done | bytes 524320 | tf_op jit(solution)/shard_map/all_to_all | solution.py:50
  76.3 17.7 %all_to_all.97 = f32[8,128,128]{2,1,0:T(8,128)S(1)} all-to-all(f32[8,128,128]{2,1,0:T(8,128)S(1)} %copy.27), channel_id=1, replica_groups=mesh['clique'=8,'shard'=4] {'clique'}, dimensions={0} | all-to-all | bytes 1048576 | tf_op jit(solution)/shard_map/all_to_all | solution.py:53
  95.0 4.4 sort.59
  99.3 8.8 %gather_fusion = s32[1024]{0:T(1024)} fusion(s32[1024]{0:T(1024)S(1)} %get-tuple-element.28, s32[1024]{0:T(1024)S(1)} %fusion.16), kind=kCustom, calls=%fused_computation | custom fusion | bytes 12288 | tf_op jit(solution)/shard_map/gather | solution.py:22
  108.1 3.2 all-to-all-start
  111.4 17.2 %all-gather.5.cloned.1.call-done = f32[4096,128]{1,0:T(8,128)} async-done(((f32[1024,128]{1,0:T(8,128)}), f32[4096,128]{1,0:T(8,128)}) %all-gather.5.cloned.1.call-update) | async-done | bytes 2097168 | tf_op jit(solution)/shard_map/all_gather | solution.py:41
  128.6 4.4 gather_fusion.3
  133.1 2.8 gather_fusion.4
  135.9 11.0 %all_to_all.98 = f32[4,256,128]{2,1,0:T(8,128)S(1)} all-to-all(f32[4,256,128]{2,1,0:T(8,128)S(1)} %bitcast.94), channel_id=1, replica_groups=mesh['clique'=8,'shard'=4] {'shard'}, dimensions={0} | all-to-all | bytes 1048576 | tf_op jit(solution)/shard_map/all_to_all | solution.py:24
  147.0 4.2 fusion.41
  151.2 9.0 %psum.29 = f32[]{:T(128)} all-reduce(f32[]{:T(128)} %get-tuple-element.36), channel_id=1, replica_groups=mesh['clique'=8,'shard'=4] {'shard'}, use_global_device_ids=true, to_apply=%region_5.6 | all-reduce | flops 1 | bytes 8 | tf_op jit(solution)/shard_map/psum | solution.py:37
  161.0 19.7 %all_to_all.99 = f32[8,128,128]{2,1,0:T(8,128)S(1)} all-to-all(f32[8,128,128]{2,1,0:T(8,128)S(1)} %bitcast.90), channel_id=1, replica_groups=mesh['clique'=8,'shard'=4] {'clique'}, dimensions={0} | all-to-all | bytes 1048576 | tf_op jit(solution)/shard_map/all_to_all | solution.py:50
  181.5 17.7 %all_to_all.100 = f32[8,128,128]{2,1,0:T(8,128)S(1)} all-to-all(f32[8,128,128]{2,1,0:T(8,128)S(1)} %copy.30), channel_id=1, replica_groups=mesh['clique'=8,'shard'=4] {'clique'}, dimensions={0} | all-to-all | bytes 1048576 | tf_op jit(solution)/shard_map/all_to_all | solution.py:53
  200.2 4.4 sort.61
  204.6 8.8 %gather_fusion.6 = s32[1024]{0:T(1024)} fusion(s32[1024]{0:T(1024)S(1)} %get-tuple-element.26, s32[1024]{0:T(1024)S(1)} %fusion.18), kind=kCustom, calls=%fused_computation.6 | custom fusion | bytes 12288 | tf_op jit(solution)/shard_map/gather | solution.py:22
  213.4 3.2 all-to-all-start.8
  216.7 17.2 %all-gather.7.cloned.1.call-done = f32[4096,128]{1,0:T(8,128)} async-done(((f32[1024,128]{1,0:T(8,128)}), f32[4096,128]{1,0:T(8,128)}) %all-gather.7.cloned.1.call-update) | async-done | bytes 2097168 | tf_op jit(solution)/shard_map/all_gather | solution.py:41
  233.9 5.6 %gather_fusion.5 = f32[1024,128]{1,0:T(8,128)} fusion(f32[4096,128]{1,0:T(8,128)} %all-gather.7.cloned.1.call-done, s32[1024]{0:T(1024)S(1)} %broadcast_clamp_fusion.2), kind=kCustom, calls=%fused_computation.5 | custom fusion | bytes 1052672 | tf_op jit(solution)/shard_map/gather | solution.py:42
  240.6 4.0 gather_fusion.7
  244.6 12.1 %all_to_all.101 = f32[4,256,128]{2,1,0:T(8,128)S(1)} all-to-all(f32[4,256,128]{2,1,0:T(8,128)} %bitcast.92), channel_id=1, replica_groups=mesh['clique'=8,'shard'=4] {'shard'}, dimensions={0} | all-to-all | bytes 1048576 | tf_op jit(solution)/shard_map/all_to_all | solution.py:24
  256.7 5.1 %fusion.42 = (f32[]{:T(128)}, f32[1024,128]{1,0:T(8,128)}) fusion(f32[1024,128]{1,0:T(8,128)S(1)} %bitcast.97, s32[1024]{0:T(1024)S(1)} %bitcast.109), kind=kOutput, calls=%fused_computation.108 | convolution fusion | flops 1611792384 | bytes 1052676 | tf_op jit(solution)/shard_map/dot_general | solution.py:30
  261.7 9.0 %psum.30 = f32[]{:T(128)} all-reduce(f32[]{:T(128)} %get-tuple-element.38), channel_id=1, replica_groups=mesh['clique'=8,'shard'=4] {'shard'}, use_global_device_ids=true, to_apply=%region_8.9 | all-reduce | flops 1 | bytes 8 | tf_op jit(solution)/shard_map/psum | solution.py:37
  272.5 19.9 %all_to_all.102 = f32[8,128,128]{2,1,0:T(8,128)S(1)} all-to-all(f32[8,128,128]{2,1,0:T(8,128)S(1)} %bitcast.88), channel_id=1, replica_groups=mesh['clique'=8,'shard'=4] {'clique'}, dimensions={0} | all-to-all | bytes 1048576 | tf_op jit(solution)/shard_map/all_to_all | solution.py:50
  293.1 17.7 %all_to_all.103 = f32[8,128,128]{2,1,0:T(8,128)S(1)} all-to-all(f32[8,128,128]{2,1,0:T(8,128)S(1)} %copy.32), channel_id=1, replica_groups=mesh['clique'=8,'shard'=4] {'clique'}, dimensions={0} | all-to-all | bytes 1048576 | tf_op jit(solution)/shard_map/all_to_all | solution.py:53
  311.8 4.4 sort.62
  316.2 8.8 %gather_fusion.9 = s32[1024]{0:T(1024)} fusion(s32[1024]{0:T(1024)S(1)} %get-tuple-element.24, s32[1024]{0:T(1024)S(1)} %fusion.19), kind=kCustom, calls=%fused_computation.9 | custom fusion | bytes 12288 | tf_op jit(solution)/shard_map/gather | solution.py:22
  325.0 3.2 all-to-all-start.12
  328.3 17.1 %all-gather.9.cloned.1.call-done = f32[4096,128]{1,0:T(8,128)} async-done(((f32[1024,128]{1,0:T(8,128)}), f32[4096,128]{1,0:T(8,128)}) %all-gather.9.cloned.1.call-update) | async-done | bytes 2097168 | tf_op jit(solution)/shard_map/all_gather | solution.py:41
  345.5 5.6 %gather_fusion.8 = f32[1024,128]{1,0:T(8,128)} fusion(f32[4096,128]{1,0:T(8,128)} %all-gather.9.cloned.1.call-done, s32[1024]{0:T(1024)S(1)} %broadcast_clamp_fusion.1), kind=kCustom, calls=%fused_computation.8 | custom fusion | bytes 1052672 | tf_op jit(solution)/shard_map/gather | solution.py:42
  352.1 2.8 gather_fusion.10
  355.0 11.0 %all_to_all.104 = f32[4,256,128]{2,1,0:T(8,128)S(1)} all-to-all(f32[4,256,128]{2,1,0:T(8,128)S(1)} %bitcast.93), channel_id=1, replica_groups=mesh['clique'=8,'shard'=4] {'shard'}, dimensions={0} | all-to-all | bytes 1048576 | tf_op jit(solution)/shard_map/all_to_all | solution.py:24
  366.0 4.3 fusion.43
  370.3 9.0 %psum.31 = f32[]{:T(128)} all-reduce(f32[]{:T(128)} %get-tuple-element.40), channel_id=1, replica_groups=mesh['clique'=8,'shard'=4] {'shard'}, use_global_device_ids=true, to_apply=%region_11.12 | all-reduce | flops 1 | bytes 8 | tf_op jit(solution)/shard_map/psum | solution.py:37
  379.9 19.9 %all_to_all.105 = f32[8,128,128]{2,1,0:T(8,128)S(1)} all-to-all(f32[8,128,128]{2,1,0:T(8,128)S(1)} %bitcast.89), channel_id=1, replica_groups=mesh['clique'=8,'shard'=4] {'clique'}, dimensions={0} | all-to-all | bytes 1048576 | tf_op jit(solution)/shard_map/all_to_all | solution.py:50
  400.6 17.7 %all_to_all.106 = f32[8,128,128]{2,1,0:T(8,128)S(1)} all-to-all(f32[8,128,128]{2,1,0:T(8,128)S(1)} %copy.34), channel_id=1, replica_groups=mesh['clique'=8,'shard'=4] {'clique'}, dimensions={0} | all-to-all | bytes 1048576 | tf_op jit(solution)/shard_map/all_to_all | solution.py:53
  419.3 33.2 %all-gather.11.cloned.1.call-done = f32[4096,128]{1,0:T(8,128)} async-done(((f32[1024,128]{1,0:T(8,128)}), f32[4096,128]{1,0:T(8,128)}) %all-gather.11.cloned.1.call-update) | async-done | bytes 2097168 | tf_op jit(solution)/shard_map/all_gather | solution.py:41
  452.5 5.6 %gather_fusion.11 = f32[1024,128]{1,0:T(8,128)} fusion(f32[4096,128]{1,0:T(8,128)} %all-gather.11.cloned.1.call-done, s32[1024]{0:T(1024)S(1)} %broadcast_clamp_fusion), kind=kCustom, calls=%fused_computation.11 | custom fusion | bytes 1052672 | tf_op jit(solution)/shard_map/gather | solution.py:42
  458.1 1.2 bitcast_multiply_fusion.4
  459.3 1.2 maximum_bitcast_fusion
  (72 shorter events, 12.1 us)
Async XLA Ops:
  11.6 14.0 %copy-start = (f32[3,1,1024,128]{3,2,1,0:T(8,128)S(1)}, f32[3,1,1024,128]{3,2,1,0:T(8,128)}, u32[]{:S(2)}) copy-start(f32[3,1,1024,128]{3,2,1,0:T(8,128)} %param.4) | copy-start | bytes 4718596
  20.5 9.9 %all-to-all-start.1 = ((s32[4,1,256]{2,1,0:T(1,128)}), s32[4,1,256]{2,1,0:T(1,128)S(1)}, u32[]{:S(2)}, u32[]{:S(2)}) async-start(s32[4,1,256]{2,1,0:T(1,128)} %bitcast.10), calls=%async_computation.1 | async-start | bytes 8192 | tf_op jit(solution)/shard_map/all_to_all | solution.py:25
  40.5 19.7 %copy-start.9 = (s32[2,8]{1,0:T(2,128)S(1)}, s32[2,8]{1,0:T(2,128)}, u32[]{:S(2)}) copy-start(s32[2,8]{1,0:T(2,128)} %param.7) | copy-start | bytes 196
  44.7 31.6 %copy-start.3 = (f32[1024,128]{1,0:T(8,128)}, f32[1024,128]{1,0:T(8,128)S(1)}, u32[]{:S(2)}) copy-start(f32[1024,128]{1,0:T(8,128)S(1)} %get-tuple-element.35) | copy-start | bytes 1572868
  55.2 20.2 %all-to-all-start.3 = ((f32[8,128,128]{2,1,0:T(8,128)}), f32[8,128,128]{2,1,0:T(8,128)S(1)}, u32[]{:S(2)}, u32[]{:S(2)}) async-start(f32[8,128,128]{2,1,0:T(8,128)} %bitcast.15), calls=%async_computation.3 | async-start | bytes 1048576 | tf_op jit(solution)/shard_map/all_to_all | solution.py:50
  60.1 68.5 %all-gather.5.cloned.1.call-start = ((), (), s32[]{:S(2)}) async-start(), calls=%async_computation.16 | async-start | bytes 2621440 | tf_op jit(solution)/shard_map/all_gather | solution.py:41
  99.3 12.1 %copy-start.7 = (s32[2,1,1024]{2,1,0:T(1,128)S(1)}, s32[2,1,1024]{2,1,0:T(1,128)}, u32[]{:S(2)}) copy-start(s32[2,1,1024]{2,1,0:T(1,128)} %param.6) | copy-start | bytes 24580
  108.1 27.8 %all-to-all-start = ((s32[4,1,256]{2,1,0:T(1,128)}), s32[4,1,256]{2,1,0:T(1,128)S(1)}, u32[]{:S(2)}, u32[]{:S(2)}) async-start(s32[4,1,256]{2,1,0:T(1,128)} %bitcast.4), calls=%async_computation | async-start | bytes 8192 | tf_op jit(solution)/shard_map/all_to_all | solution.py:25
  111.3 122.6 %all-gather.7.cloned.1.call-start = ((), (), s32[]{:S(2)}) async-start(), calls=%async_computation.17 | async-start | bytes 2621440 | tf_op jit(solution)/shard_map/all_gather | solution.py:41
  151.2 30.4 %copy-start.5 = (f32[1024,128]{1,0:T(8,128)}, f32[1024,128]{1,0:T(8,128)S(1)}, u32[]{:S(2)}) copy-start(f32[1024,128]{1,0:T(8,128)S(1)} %get-tuple-element.37) | copy-start | bytes 1572868
  213.4 31.2 %all-to-all-start.8 = ((s32[4,1,256]{2,1,0:T(1,128)}), s32[4,1,256]{2,1,0:T(1,128)S(1)}, u32[]{:S(2)}, u32[]{:S(2)}) async-start(s32[4,1,256]{2,1,0:T(1,128)} %bitcast.30), calls=%async_computation.8 | async-start | bytes 8192 | tf_op jit(solution)/shard_map/all_to_all | solution.py:25
  216.7 128.8 %all-gather.9.cloned.1.call-start = ((), (), s32[]{:S(2)}) async-start(), calls=%async_computation.18 | async-start | bytes 2621440 | tf_op jit(solution)/shard_map/all_gather | solution.py:41
  272.4 38.4 %copy-start.6 = (f32[1024,128]{1,0:T(8,128)S(1)}, f32[1024,128]{1,0:T(8,128)}, u32[]{:S(2)}) copy-start(f32[1024,128]{1,0:T(8,128)} %copy-done.5) | copy-start | bytes 1572868
  316.2 12.1 %copy-start.8 = (s32[2,1,1024]{2,1,0:T(1,128)S(1)}, s32[2,1,1024]{2,1,0:T(1,128)}, u32[]{:S(2)}) copy-start(s32[2,1,1024]{2,1,0:T(1,128)} %param.5) | copy-start | bytes 24580
  325.0 30.0 %all-to-all-start.12 = ((s32[4,1,256]{2,1,0:T(1,128)}), s32[4,1,256]{2,1,0:T(1,128)S(1)}, u32[]{:S(2)}, u32[]{:S(2)}) async-start(s32[4,1,256]{2,1,0:T(1,128)} %bitcast.43), calls=%async_computation.12 | async-start | bytes 8192 | tf_op jit(solution)/shard_map/all_to_all | solution.py:25
  328.2 124.2 %all-gather.11.cloned.1.call-start = ((), (), s32[]{:S(2)}) async-start(), calls=%async_computation.19 | async-start | bytes 2621440 | tf_op jit(solution)/shard_map/all_gather | solution.py:41
  379.9 38.4 %copy-start.4 = (f32[1024,128]{1,0:T(8,128)S(1)}, f32[1024,128]{1,0:T(8,128)}, u32[]{:S(2)}) copy-start(f32[1024,128]{1,0:T(8,128)} %copy-done.3) | copy-start | bytes 1572868
  419.2 38.8 %copy-start.1 = (f32[1024,128]{1,0:T(8,128)S(1)}, f32[1024,128]{1,0:T(8,128)}, u32[]{:S(2)}) copy-start(f32[1024,128]{1,0:T(8,128)} %gather_fusion.5) | copy-start | bytes 1572868
  419.3 38.8 %copy-start.2 = (f32[1024,128]{1,0:T(8,128)S(1)}, f32[1024,128]{1,0:T(8,128)}, u32[]{:S(2)}) copy-start(f32[1024,128]{1,0:T(8,128)} %gather_fusion.8) | copy-start | bytes 1572868
Sparse Core Ops, SparseCore 0:
  95.1 33.5 all-gather.4
  200.3 33.5 all-gather.6
  311.9 33.5 all-gather.8
  419.4 33.0 all-gather.10
where the time goes:
time: 468 us; the launch traced here: 467 us
  blocking collectives  211 us (45%)
  waiting for transfers between devices  102 us (22%)
  local copies, waits for them, and re-layouts  71.8 us (15%)
  other arithmetic  26.1 us (6%)
  matrix products  20.5 us (4%)
  starting transfers between devices  19.9 us (4%)
  between operations  16.1 us (3%)
    all_gather x4, waiting for transfers between devices, fetch(): gathered = lax.all_gather(owned_rows, 'shard', axis=0, tiled=True)  84.7 us
    all_to_all x4, blocking collectives, route(): lax.all_to_all(combined, 'clique', split_axis=0, concat_axis=0, tiled=True)  70.9 us
    all_to_all x3, blocking collectives, route(): lax.all_to_all(pieces, 'clique', split_axis=0, concat_axis=0, tiled=True)  59.5 us
    all_to_all x4, blocking collectives, to_owners(): lax.all_to_all(sent_rows, 'shard', split_axis=0, concat_axis=0, tiled=True)  44.3 us
    psum x4, blocking collectives, to_owners(): total = lax.psum(partial_sum, 'shard')  36 us
    gather x4, local copies, waits for them, and re-layouts, to_owners(): (index_list % per_owner)[ordering].reshape(shard_count, per_peer)  35.3 us
    gather x4, local copies, waits for them, and re-layouts, fetch(): result = gathered[index_list]  21.2 us
    dot_general x4, matrix products, to_owners(): jnp.dot(one_hot.T, arrived_rows.reshape(block_count, lane_count), precisi...  17.8 us
  transfers between devices with their start and end apart: 9, of which 6 were waited for; matrix products, arithmetic and copies ran while one was open for 15% of the time, Pallas kernels for 0%

commit v1 on v0

--- a/solution.py
+++ b/solution.py
@@ -38,7 +38,12 @@
         return message * (sep_states / total)
 
     def fetch(owned_rows, index_list):
-        gathered = lax.all_gather(owned_rows, "shard", axis=0, tiled=True)
+        gathered = jnp.concatenate(
+            lax.all_to_all(
+                jnp.stack(tuple((owned_rows for _ in range(lax.psum(1, "shard"))))), "shard", 0, 0
+            ),
+            axis=0,
+        )
         result = gathered[index_list]
         return result
 

time: 468 us -> 437 us (0.934)
  waiting for transfers between devices: 102 us -> 75.3 us
  starting transfers between devices: 19.9 us -> 34.2 us
  between operations: 16.1 us -> 2.99 us
    all_gather x4 -> x0, waiting for transfers between devices: 84.7 us -> none  [fetch(): gathered = lax.all_gather(owned_rows, 'shard', axis=0, tiled=True)]
    all_to_all x0 -> x4, waiting for transfers between devices: none -> 59.2 us  [fetch(): lax.all_to_all(jnp.stack(tuple((owned_rows for _ in range(lax.psum(1, 'sh...]
    all_to_all x0 -> x4, starting transfers between devices: none -> 14.4 us  [fetch(): lax.all_to_all(jnp.stack(tuple((owned_rows for _ in range(lax.psum(1, 'sh...]
    gather x4, local copies, waits for them, and re-layouts: 21.2 us -> 14.8 us  [fetch(): result = gathered[index_list]]
    another operation x0 -> x4, local copies, waits for them, and re-layouts: none -> 5.95 us  [fetch(): jnp.stack(tuple((owned_rows for _ in range(lax.psum(1, 'shard')))))]
where the time goes in v1:
time: 437 us; the launch traced here: 435 us
  blocking collectives  208 us (48%)
  waiting for transfers between devices  75.3 us (17%)
  local copies, waits for them, and re-layouts  69.8 us (16%)
  starting transfers between devices  34.2 us (8%)
  other arithmetic  25.4 us (6%)
  matrix products  19.8 us (5%)
    all_to_all x4, blocking collectives, route(): lax.all_to_all(combined, 'clique', split_axis=0, concat_axis=0, tiled=True)  70.9 us
    all_to_all x4, waiting for transfers between devices, fetch(): lax.all_to_all(jnp.stack(tuple((owned_rows for _ in range(lax.psum(1, 'sh...  59.2 us
    all_to_all x3, blocking collectives, route(): lax.all_to_all(pieces, 'clique', split_axis=0, concat_axis=0, tiled=True)  55.5 us
    all_to_all x4, blocking collectives, to_owners(): lax.all_to_all(sent_rows, 'shard', split_axis=0, concat_axis=0, tiled=True)  45.4 us
    psum x4, blocking collectives, to_owners(): total = lax.psum(partial_sum, 'shard')  35.9 us
    gather x4, local copies, waits for them, and re-layouts, to_owners(): (index_list % per_owner)[ordering].reshape(shard_count, per_peer)  35.3 us
    sort x4, other arithmetic, to_owners(): ordering = jnp.argsort(index_list // per_owner, stable=True)  17.5 us
    dot_general x4, matrix products, to_owners(): jnp.dot(one_hot.T, arrived_rows.reshape(block_count, lane_count), precisi...  17 us
  transfers between devices with their start and end apart: 9, of which 6 were waited for; matrix products, arithmetic and copies ran while one was open for 15% of the time, Pallas kernels for 0%

profile of v1, /device:TPU:0, one launch (start us, length us, event | category | flops | bytes accessed | tf_op | source)
XLA Modules:
  0.0 435.2 jit_solution(1123531803942842145)
XLA Ops:
  0.7 4.4 %sort.60 = (s32[1024]{0:T(1024)}, s32[1024]{0:T(1024)S(1)}) sort(s32[1024]{0:T(1024)S(1)} %get-tuple-element.31, s32[1024]{0:T(1024)S(1)} %iota.22), dimensions={0}, to_apply=%region_1.2 | sort | flops 10240 | bytes 16384 | tf_op jit(solution)/shard_map/jit(argsort)/sort | solution.py:20
  5.1 8.8 %gather_fusion.1 = s32[1024]{0:T(1024)} fusion(s32[1024]{0:T(1024)S(1)} %get-tuple-element.30, s32[1024]{0:T(1024)S(1)} %fusion.17), kind=kCustom, calls=%fused_computation.1 | custom fusion | bytes 12288 | tf_op jit(solution)/shard_map/gather | solution.py:22
  13.9 5.2 %all-to-all-start.1 = ((s32[4,1,256]{2,1,0:T(1,128)}), s32[4,1,256]{2,1,0:T(1,128)S(1)}, u32[]{:S(2)}, u32[]{:S(2)}) async-start(s32[4,1,256]{2,1,0:T(1,128)} %bitcast.10), calls=%async_computation.1 | async-start | bytes 8192 | tf_op jit(solution)/shard_map/all_to_all | solution.py:25
  20.2 2.8 gather_fusion.2
  23.8 11.2 %all_to_all.116 = f32[4,256,128]{2,1,0:T(8,128)S(1)} all-to-all(f32[4,256,128]{2,1,0:T(8,128)S(1)} %bitcast.99), channel_id=1, replica_groups=mesh['clique'=8,'shard'=4] {'shard'}, dimensions={0} | all-to-all | bytes 1048576 | tf_op jit(solution)/shard_map/all_to_all | solution.py:24
  35.0 4.2 fusion.40
  39.2 9.0 %psum.28 = f32[]{:T(128)} all-reduce(f32[]{:T(128)} %get-tuple-element.34), channel_id=1, replica_groups=mesh['clique'=8,'shard'=4] {'shard'}, use_global_device_ids=true, to_apply=%region_3.4 | all-reduce | flops 1 | bytes 8 | tf_op jit(solution)/shard_map/psum | solution.py:37
  49.7 4.9 %all-to-all-start.3 = ((f32[8,128,128]{2,1,0:T(8,128)}), f32[8,128,128]{2,1,0:T(8,128)S(1)}, u32[]{:S(2)}, u32[]{:S(2)}) async-start(f32[8,128,128]{2,1,0:T(8,128)} %bitcast.15), calls=%async_computation.3 | async-start | bytes 1048576 | tf_op jit(solution)/shard_map/all_to_all | solution.py:55
  54.6 15.3 %all-to-all-done.3 = f32[8,128,128]{2,1,0:T(8,128)S(1)} async-done(((f32[8,128,128]{2,1,0:T(8,128)}), f32[8,128,128]{2,1,0:T(8,128)S(1)}, u32[]{:S(2)}, u32[]{:S(2)}) %all-to-all-start.3) | async-done | bytes 524320 | tf_op jit(solution)/shard_map/all_to_all | solution.py:55
  70.8 17.7 %all_to_all.117 = f32[8,128,128]{2,1,0:T(8,128)S(1)} all-to-all(f32[8,128,128]{2,1,0:T(8,128)S(1)} %copy.27), channel_id=1, replica_groups=mesh['clique'=8,'shard'=4] {'clique'}, dimensions={0} | all-to-all | bytes 1048576 | tf_op jit(solution)/shard_map/all_to_all | solution.py:58
  90.1 3.6 all-to-all-start.5
  93.8 4.4 %sort.59 = (s32[1024]{0:T(1024)}, s32[1024]{0:T(1024)S(1)}) sort(s32[1024]{0:T(1024)S(1)} %get-tuple-element.29, s32[1024]{0:T(1024)S(1)} %iota.21), dimensions={0}, to_apply=%region_0.1 | sort | flops 10240 | bytes 16384 | tf_op jit(solution)/shard_map/jit(argsort)/sort | solution.py:20
  98.1 8.8 %gather_fusion = s32[1024]{0:T(1024)} fusion(s32[1024]{0:T(1024)S(1)} %get-tuple-element.28, s32[1024]{0:T(1024)S(1)} %fusion.16), kind=kCustom, calls=%fused_computation | custom fusion | bytes 12288 | tf_op jit(solution)/shard_map/gather | solution.py:22
  107.0 11.5 %all-to-all-done.5 = f32[4,1024,128]{2,1,0:T(8,128)S(1)} async-done(((f32[4,1024,128]{2,1,0:T(8,128)}), f32[4,1024,128]{2,1,0:T(8,128)S(1)}, u32[]{:S(2)}, u32[]{:S(2)}) %all-to-all-start.5) | async-done | bytes 2097184 | tf_op jit(solution)/shard_map/all_to_all | solution.py:42
  118.5 3.2 all-to-all-start
  121.7 2.8 gather_fusion.3
  128.5 11.4 %all_to_all.118 = f32[4,256,128]{2,1,0:T(8,128)S(1)} all-to-all(f32[4,256,128]{2,1,0:T(8,128)S(1)} %bitcast.102), channel_id=1, replica_groups=mesh['clique'=8,'shard'=4] {'shard'}, dimensions={0} | all-to-all | bytes 1048576 | tf_op jit(solution)/shard_map/all_to_all | solution.py:24
  139.9 4.2 fusion.41
  144.1 9.0 %psum.29 = f32[]{:T(128)} all-reduce(f32[]{:T(128)} %get-tuple-element.36), channel_id=1, replica_groups=mesh['clique'=8,'shard'=4] {'shard'}, use_global_device_ids=true, to_apply=%region_5.6 | all-reduce | flops 1 | bytes 8 | tf_op jit(solution)/shard_map/psum | solution.py:37
  153.9 18.4 %all_to_all.119 = f32[8,128,128]{2,1,0:T(8,128)S(1)} all-to-all(f32[8,128,128]{2,1,0:T(8,128)S(1)} %bitcast.98), channel_id=1, replica_groups=mesh['clique'=8,'shard'=4] {'clique'}, dimensions={0} | all-to-all | bytes 1048576 | tf_op jit(solution)/shard_map/all_to_all | solution.py:55
  173.2 17.7 %all_to_all.120 = f32[8,128,128]{2,1,0:T(8,128)S(1)} all-to-all(f32[8,128,128]{2,1,0:T(8,128)S(1)} %copy.30), channel_id=1, replica_groups=mesh['clique'=8,'shard'=4] {'clique'}, dimensions={0} | all-to-all | bytes 1048576 | tf_op jit(solution)/shard_map/all_to_all | solution.py:58
  192.5 3.6 all-to-all-start.9
  196.1 4.4 %sort.61 = (s32[1024]{0:T(1024)}, s32[1024]{0:T(1024)S(1)}) sort(s32[1024]{0:T(1024)S(1)} %get-tuple-element.27, s32[1024]{0:T(1024)S(1)} %iota.23), dimensions={0}, to_apply=%region_6.7 | sort | flops 10240 | bytes 16384 | tf_op jit(solution)/shard_map/jit(argsort)/sort | solution.py:20
  200.5 8.8 %gather_fusion.6 = s32[1024]{0:T(1024)} fusion(s32[1024]{0:T(1024)S(1)} %get-tuple-element.26, s32[1024]{0:T(1024)S(1)} %fusion.18), kind=kCustom, calls=%fused_computation.6 | custom fusion | bytes 12288 | tf_op jit(solution)/shard_map/gather | solution.py:22
  209.3 11.5 %all-to-all-done.9 = f32[4,1024,128]{2,1,0:T(8,128)S(1)} async-done(((f32[4,1024,128]{2,1,0:T(8,128)}), f32[4,1024,128]{2,1,0:T(8,128)S(1)}, u32[]{:S(2)}, u32[]{:S(2)}) %all-to-all-start.9) | async-done | bytes 2097184 | tf_op jit(solution)/shard_map/all_to_all | solution.py:42
  220.8 3.2 all-to-all-start.10
  224.1 4.0 gather_fusion.5
  229.4 2.8 gather_fusion.7
  232.2 11.4 %all_to_all.121 = f32[4,256,128]{2,1,0:T(8,128)S(1)} all-to-all(f32[4,256,128]{2,1,0:T(8,128)S(1)} %bitcast.100), channel_id=1, replica_groups=mesh['clique'=8,'shard'=4] {'shard'}, dimensions={0} | all-to-all | bytes 1048576 | tf_op jit(solution)/shard_map/all_to_all | solution.py:24
  243.6 4.3 fusion.42
  247.9 9.0 %psum.30 = f32[]{:T(128)} all-reduce(f32[]{:T(128)} %get-tuple-element.38), channel_id=1, replica_groups=mesh['clique'=8,'shard'=4] {'shard'}, use_global_device_ids=true, to_apply=%region_8.9 | all-reduce | flops 1 | bytes 8 | tf_op jit(solution)/shard_map/psum | solution.py:37
  257.5 18.5 %all_to_all.122 = f32[8,128,128]{2,1,0:T(8,128)S(1)} all-to-all(f32[8,128,128]{2,1,0:T(8,128)S(1)} %bitcast.96), channel_id=1, replica_groups=mesh['clique'=8,'shard'=4] {'clique'}, dimensions={0} | all-to-all | bytes 1048576 | tf_op jit(solution)/shard_map/all_to_all | solution.py:55
  276.9 17.7 %all_to_all.123 = f32[8,128,128]{2,1,0:T(8,128)S(1)} all-to-all(f32[8,128,128]{2,1,0:T(8,128)S(1)} %copy.32), channel_id=1, replica_groups=mesh['clique'=8,'shard'=4] {'clique'}, dimensions={0} | all-to-all | bytes 1048576 | tf_op jit(solution)/shard_map/all_to_all | solution.py:58
  296.2 3.6 all-to-all-start.14
  299.8 4.4 %sort.62 = (s32[1024]{0:T(1024)}, s32[1024]{0:T(1024)S(1)}) sort(s32[1024]{0:T(1024)S(1)} %get-tuple-element.25, s32[1024]{0:T(1024)S(1)} %iota.24), dimensions={0}, to_apply=%region_9.10 | sort | flops 10240 | bytes 16384 | tf_op jit(solution)/shard_map/jit(argsort)/sort | solution.py:20
  304.2 8.8 %gather_fusion.9 = s32[1024]{0:T(1024)} fusion(s32[1024]{0:T(1024)S(1)} %get-tuple-element.24, s32[1024]{0:T(1024)S(1)} %fusion.19), kind=kCustom, calls=%fused_computation.9 | custom fusion | bytes 12288 | tf_op jit(solution)/shard_map/gather | solution.py:22
  313.0 11.5 %all-to-all-done.14 = f32[4,1024,128]{2,1,0:T(8,128)S(1)} async-done(((f32[4,1024,128]{2,1,0:T(8,128)}), f32[4,1024,128]{2,1,0:T(8,128)S(1)}, u32[]{:S(2)}, u32[]{:S(2)}) %all-to-all-start.14) | async-done | bytes 2097184 | tf_op jit(solution)/shard_map/all_to_all | solution.py:42
  324.5 3.2 all-to-all-start.15
  327.8 4.0 gather_fusion.8
  332.9 2.8 gather_fusion.10
  335.7 11.4 %all_to_all.124 = f32[4,256,128]{2,1,0:T(8,128)S(1)} all-to-all(f32[4,256,128]{2,1,0:T(8,128)S(1)} %bitcast.101), channel_id=1, replica_groups=mesh['clique'=8,'shard'=4] {'shard'}, dimensions={0} | all-to-all | bytes 1048576 | tf_op jit(solution)/shard_map/all_to_all | solution.py:24
  347.1 4.3 fusion.43
  351.4 9.0 %psum.31 = f32[]{:T(128)} all-reduce(f32[]{:T(128)} %get-tuple-element.40), channel_id=1, replica_groups=mesh['clique'=8,'shard'=4] {'shard'}, use_global_device_ids=true, to_apply=%region_11.12 | all-reduce | flops 1 | bytes 8 | tf_op jit(solution)/shard_map/psum | solution.py:37
  361.1 18.5 %all_to_all.125 = f32[8,128,128]{2,1,0:T(8,128)S(1)} all-to-all(f32[8,128,128]{2,1,0:T(8,128)S(1)} %bitcast.97), channel_id=1, replica_groups=mesh['clique'=8,'shard'=4] {'clique'}, dimensions={0} | all-to-all | bytes 1048576 | tf_op jit(solution)/shard_map/all_to_all | solution.py:55
  380.4 17.7 %all_to_all.126 = f32[8,128,128]{2,1,0:T(8,128)S(1)} all-to-all(f32[8,128,128]{2,1,0:T(8,128)S(1)} %copy.34), channel_id=1, replica_groups=mesh['clique'=8,'shard'=4] {'clique'}, dimensions={0} | all-to-all | bytes 1048576 | tf_op jit(solution)/shard_map/all_to_all | solution.py:58
  399.7 3.6 all-to-all-start.19
  403.3 24.7 %all-to-all-done.19 = f32[4,1024,128]{2,1,0:T(8,128)S(1)} async-done(((f32[4,1024,128]{2,1,0:T(8,128)}), f32[4,1024,128]{2,1,0:T(8,128)S(1)}, u32[]{:S(2)}, u32[]{:S(2)}) %all-to-all-start.19) | async-done | bytes 2097184 | tf_op jit(solution)/shard_map/all_to_all | solution.py:42
  428.1 4.0 gather_fusion.11
  (68 shorter events, 22.6 us)
Async XLA Ops:
  13.9 9.9 %all-to-all-start.1 = ((s32[4,1,256]{2,1,0:T(1,128)}), s32[4,1,256]{2,1,0:T(1,128)S(1)}, u32[]{:S(2)}, u32[]{:S(2)}) async-start(s32[4,1,256]{2,1,0:T(1,128)} %bitcast.10), calls=%async_computation.1 | async-start | bytes 8192 | tf_op jit(solution)/shard_map/all_to_all | solution.py:25
  35.0 19.6 %copy-start.7 = (s32[2,8]{1,0:T(2,128)S(1)}, s32[2,8]{1,0:T(2,128)}, u32[]{:S(2)}) copy-start(s32[2,8]{1,0:T(2,128)} %param.7) | copy-start | bytes 196
  39.2 31.6 %copy-start.1 = (f32[1024,128]{1,0:T(8,128)}, f32[1024,128]{1,0:T(8,128)S(1)}, u32[]{:S(2)}) copy-start(f32[1024,128]{1,0:T(8,128)S(1)} %get-tuple-element.35) | copy-start | bytes 1572868
  49.7 20.2 %all-to-all-start.3 = ((f32[8,128,128]{2,1,0:T(8,128)}), f32[8,128,128]{2,1,0:T(8,128)S(1)}, u32[]{:S(2)}, u32[]{:S(2)}) async-start(f32[8,128,128]{2,1,0:T(8,128)} %bitcast.15), calls=%async_computation.3 | async-start | bytes 1048576 | tf_op jit(solution)/shard_map/all_to_all | solution.py:55
  90.1 28.4 %all-to-all-start.5 = ((f32[4,1024,128]{2,1,0:T(8,128)}), f32[4,1024,128]{2,1,0:T(8,128)S(1)}, u32[]{:S(2)}, u32[]{:S(2)}) async-start(f32[4,1024,128]{2,1,0:T(8,128)} %stack.10), calls=%async_computation.5 | async-start | bytes 4194304 | tf_op jit(solution)/shard_map/all_to_all | solution.py:42
  98.1 8.8 %copy-start.5 = (s32[2,1,1024]{2,1,0:T(1,128)S(1)}, s32[2,1,1024]{2,1,0:T(1,128)}, u32[]{:S(2)}) copy-start(s32[2,1,1024]{2,1,0:T(1,128)} %param.6) | copy-start | bytes 24580
  118.5 10.0 %all-to-all-start = ((s32[4,1,256]{2,1,0:T(1,128)}), s32[4,1,256]{2,1,0:T(1,128)S(1)}, u32[]{:S(2)}, u32[]{:S(2)}) async-start(s32[4,1,256]{2,1,0:T(1,128)} %bitcast.4), calls=%async_computation | async-start | bytes 8192 | tf_op jit(solution)/shard_map/all_to_all | solution.py:25
  144.1 29.0 %copy-start.3 = (f32[1024,128]{1,0:T(8,128)}, f32[1024,128]{1,0:T(8,128)S(1)}, u32[]{:S(2)}) copy-start(f32[1024,128]{1,0:T(8,128)S(1)} %get-tuple-element.37) | copy-start | bytes 1572868
  192.5 28.4 %all-to-all-start.9 = ((f32[4,1024,128]{2,1,0:T(8,128)}), f32[4,1024,128]{2,1,0:T(8,128)S(1)}, u32[]{:S(2)}, u32[]{:S(2)}) async-start(f32[4,1024,128]{2,1,0:T(8,128)} %stack.11), calls=%async_computation.9 | async-start | bytes 4194304 | tf_op jit(solution)/shard_map/all_to_all | solution.py:42
  220.8 11.4 %all-to-all-start.10 = ((s32[4,1,256]{2,1,0:T(1,128)}), s32[4,1,256]{2,1,0:T(1,128)S(1)}, u32[]{:S(2)}, u32[]{:S(2)}) async-start(s32[4,1,256]{2,1,0:T(1,128)} %bitcast.32), calls=%async_computation.10 | async-start | bytes 8192 | tf_op jit(solution)/shard_map/all_to_all | solution.py:25
  257.5 37.1 %copy-start.4 = (f32[1024,128]{1,0:T(8,128)S(1)}, f32[1024,128]{1,0:T(8,128)}, u32[]{:S(2)}) copy-start(f32[1024,128]{1,0:T(8,128)} %copy-done.3) | copy-start | bytes 1572868
  296.2 28.4 %all-to-all-start.14 = ((f32[4,1024,128]{2,1,0:T(8,128)}), f32[4,1024,128]{2,1,0:T(8,128)S(1)}, u32[]{:S(2)}, u32[]{:S(2)}) async-start(f32[4,1024,128]{2,1,0:T(8,128)} %stack.12), calls=%async_computation.14 | async-start | bytes 4194304 | tf_op jit(solution)/shard_map/all_to_all | solution.py:42
  304.2 8.8 %copy-start.6 = (s32[2,1,1024]{2,1,0:T(1,128)S(1)}, s32[2,1,1024]{2,1,0:T(1,128)}, u32[]{:S(2)}) copy-start(s32[2,1,1024]{2,1,0:T(1,128)} %param.5) | copy-start | bytes 24580
  324.5 11.2 %all-to-all-start.15 = ((s32[4,1,256]{2,1,0:T(1,128)}), s32[4,1,256]{2,1,0:T(1,128)S(1)}, u32[]{:S(2)}, u32[]{:S(2)}) async-start(s32[4,1,256]{2,1,0:T(1,128)} %bitcast.46), calls=%async_computation.15 | async-start | bytes 8192 | tf_op jit(solution)/shard_map/all_to_all | solution.py:25
  361.1 37.1 %copy-start.2 = (f32[1024,128]{1,0:T(8,128)S(1)}, f32[1024,128]{1,0:T(8,128)}, u32[]{:S(2)}) copy-start(f32[1024,128]{1,0:T(8,128)} %copy-done.1) | copy-start | bytes 1572868
  399.7 28.4 %all-to-all-start.19 = ((f32[4,1024,128]{2,1,0:T(8,128)}), f32[4,1024,128]{2,1,0:T(8,128)S(1)}, u32[]{:S(2)}, u32[]{:S(2)}) async-start(f32[4,1024,128]{2,1,0:T(8,128)} %stack.13), calls=%async_computation.19 | async-start | bytes 4194304 | tf_op jit(solution)/shard_map/all_to_all | solution.py:42
  428.1 4.0 copy-start
